TPU v7x, 128 devices: a whole 4x4x4 slice. The times are simulated.
128 devices in a mesh: fsdp: 32 (over y, z, core), seq: 4 (over x).
Axes of the slice: x: 4, y: 4, z: 4, core: 2. Of those that a mesh axis runs over, the one named last changes fastest.
Arguments:
- draft_tokens: bfloat16 [32768, 2048], P('fsdp'), may hold values from -6 to 6
- draft_gate: bfloat16 [2048, 4096], P('fsdp', 'seq'), may hold values from -0.125 to 0.125
- draft_up: bfloat16 [2048, 4096], P('fsdp', 'seq'), may hold values from -0.125 to 0.125
- draft_head: float32 [4096], P('seq'), may hold values from -0.75 to 0.75
- verifier_rows: bfloat16 [32768, 8192], P(('fsdp', 'seq')), may hold values from -6 to 6
- norm_gain: float32 [8192], replicated, may hold values from 0.5 to 1.5
- key_weight: bfloat16 [8192, 512], P('fsdp'), may hold values from -0.06629126 to 0.06629126
- value_weight: bfloat16 [8192, 512], P('fsdp'), may hold values from -0.0625 to 0.0625
- pool_query: float32 [4, 4, 128], replicated, may hold values from -32 to 32
- flags: int32 [1024], P(('fsdp', 'seq')), may hold values from 0 to 1, as said below
- owner: int32 [1024], P(('fsdp', 'seq')), may hold values from 0 to 3
Outputs:
- draft_score: float32 [1024], P(('fsdp', 'seq'))
- verdict: bfloat16 [1024, 512], P(('fsdp', 'seq'))
Inputs may be any that keep to these rules, and one draw needn't show every extreme that they name: `flags`: on the 8 segments of one device, at most 4 flagged segments share an owner lane, and on every device exactly 4 flagged segments share one lane.
All inputs are finite; a program needn't handle non-finite values.
Results may differ from a plain program's by a relative error of at most 0.009.
Values may be sent and summed in bfloat16 or wider, within the bound.
No kernel may reach another device: no remote copies, remote signals or barrier semaphores. Data moves between devices by JAX's collectives and lax.ppermute only.
A program may use at most 128 MiB of HBM per device.

v0:
```python
import math
import jax
import jax.numpy as jnp
from jax import lax
from jax.sharding import PartitionSpec as P

KVH = 4
HD = 128
SEGL = 32
eps = 1e-05


def normalize_rows(rows, norm_gain):
    values = rows.astype(jnp.float32)
    scale = lax.rsqrt(jnp.mean(values * values, axis=-1, keepdims=True) + eps)
    return (values * scale * norm_gain).astype(jnp.bfloat16)


def segment_pool(seg_keys, seg_values, queries, head_size):
    scores = jnp.einsum(
        "sthd,shd->sth", seg_keys, queries, precision=lax.Precision.HIGHEST
    ) / math.sqrt(head_size)
    scores = scores - jnp.max(scores, axis=1, keepdims=True)
    weights = jnp.exp(scores)
    weights = weights / jnp.sum(weights, axis=1, keepdims=True)
    summary_key = jnp.einsum("sth,sthd->shd", weights, seg_keys, precision=lax.Precision.HIGHEST)
    summary_value = jnp.einsum(
        "sth,sthd->shd", weights, seg_values, precision=lax.Precision.HIGHEST
    )
    return (summary_key, summary_value)


def cross_pool(query_keys, key_all, value_all, live_all, head_size):
    scores = jnp.einsum(
        "jhd,ihd->jhi", query_keys, key_all, precision=lax.Precision.HIGHEST
    ) / math.sqrt(head_size)
    scores = jnp.where(live_all[None, None, :], scores, -1e30)
    highest = jnp.max(scores, axis=2, keepdims=True)
    weights = jnp.where(live_all[None, None, :], jnp.exp(scores - highest), 0.0)
    total = jnp.sum(weights, axis=2, keepdims=True)
    return jnp.einsum("jhi,ihd->jhd", weights, value_all, precision=lax.Precision.HIGHEST) / total


def project_pair(row_block, pieces):
    return (
        jnp.dot(row_block, pieces[0], preferred_element_type=jnp.float32),
        jnp.dot(row_block, pieces[1], preferred_element_type=jnp.float32),
    )


def local(
    draft_tokens,
    draft_gate,
    draft_up,
    draft_head,
    verifier_rows,
    norm_gain,
    key_weight,
    value_weight,
    pool_query,
    flags,
    owner,
):
    seg_count = flags.shape[0]
    gate, upward = project_pair(
        draft_tokens,
        (
            lax.all_gather(draft_gate, "fsdp", axis=0, tiled=True),
            lax.all_gather(draft_up, "fsdp", axis=0, tiled=True),
        ),
    )
    partial_scores = jnp.sum(jax.nn.silu(gate) * upward * draft_head[None, :], axis=1)
    own_scores = lax.psum_scatter(partial_scores, "seq", scatter_dimension=0, tiled=True)
    draft_score = jnp.mean(own_scores.reshape(seg_count, SEGL), axis=1)
    normed = normalize_rows(verifier_rows, norm_gain)
    seg_keys, seg_values = project_pair(
        normed,
        (
            lax.all_gather(key_weight, "fsdp", axis=0, tiled=True),
            lax.all_gather(value_weight, "fsdp", axis=0, tiled=True),
        ),
    )
    lane_pick = (
        owner[:, None] == jnp.arange(pool_query.shape[0], dtype=jnp.int32)[None, :]
    ).astype(jnp.float32)
    queries = jnp.einsum("sc,chd->shd", lane_pick, pool_query, precision=lax.Precision.HIGHEST)
    summary_key, summary_value = segment_pool(
        seg_keys.reshape(seg_count, SEGL, KVH, HD),
        seg_values.reshape(seg_count, SEGL, KVH, HD),
        queries,
        HD,
    )
    live_own = flags.astype(jnp.float32)
    key_all, value_all, live_all = (
        lax.all_gather(summary_key.reshape(seg_count, KVH * HD), "seq", axis=0, tiled=True),
        lax.all_gather(summary_value.reshape(seg_count, KVH * HD), "seq", axis=0, tiled=True),
        lax.all_gather(live_own, "seq", axis=0, tiled=True),
    )
    pooled = cross_pool(
        summary_key,
        key_all.reshape(-1, KVH, HD),
        value_all.reshape(-1, KVH, HD),
        live_all > 0.5,
        HD,
    )
    own_pooled = pooled.reshape(seg_count, KVH * HD)
    verdict = jnp.where(
        flags[:, None] == 1, jax.nn.sigmoid(draft_score)[:, None] * own_pooled, 0.0
    ).astype(jnp.bfloat16)
    return (draft_score, verdict)


def solution(mesh):
    return jax.shard_map(
        local,
        mesh=mesh,
        in_specs=(
            P("fsdp", None),
            P("fsdp", "seq"),
            P("fsdp", "seq"),
            P("seq"),
            P(("fsdp", "seq"), None),
            P(),
            P("fsdp", None),
            P("fsdp", None),
            P(),
            P(("fsdp", "seq")),
            P(("fsdp", "seq")),
        ),
        out_specs=(P(("fsdp", "seq")), P(("fsdp", "seq"), None)),
        check_vma=False,
    )
```

profile of v0, /device:TPU:0, one launch (start us, length us, event | category | flops | bytes accessed | tf_op | source)
XLA Modules:
  0.0 243.5 jit_solution(6076633560900266448)
XLA Ops:
  7.2 0.7 all-gather.5.cloned.1.call-update
  8.0 0.7 all-gather.7.cloned.1.call-update
  8.7 0.7 all-gather.9.cloned.1.call-update
  9.4 0.5 all-gather.11.cloned.1.call-update
  10.0 1.3 fusion.44
  12.6 0.9 convolution_bitcast_fusion.1
  13.5 0.7 broadcast_compare_fusion.1
  14.1 0.7 convert_dynamic-update-slice_fusion
  14.9 3.1 %fusion.1 = f32[256]{0:T(256)S(1)} fusion(bf16[256,8192]{1,0:T(8,128)(2,1)} %param.15), kind=kLoop, calls=%fused_computation.3 | loop fusion | flops 6291200 | bytes 4195328 | tf_op jit(solution)/shard_map/reduce_sum | solution.py:15
  18.0 41.0 %all-gather.5.cloned.1.call-done = bf16[2048,1024]{1,0:T(8,128)(2,1)} async-done(((bf16[64,1024]{1,0:T(8,128)(2,1)}), bf16[2048,1024]{1,0:T(8,128)(2,1)}) %all-gather.5.cloned.1.call-update) | async-done | bytes 4194320 | tf_op jit(solution)/shard_map/all_gather | solution.py:68
  59.0 10.0 %fusion.47 = f32[1024,1024]{0,1:T(8,128)} fusion(bf16[1024,2048]{1,0:T(8,128)(2,1)} %param.11, bf16[2048,1024]{1,0:T(8,128)(2,1)} %all-gather.5.cloned.1.call-done), kind=kOutput, calls=%fused_computation.63 | convolution fusion | flops 4294967296 | bytes 12582912 | tf_op jit(solution)/shard_map/dot_general | solution.py:46
  69.0 37.8 %all-gather.7.cloned.1.call-done = bf16[2048,1024]{1,0:T(8,128)(2,1)} async-done(((bf16[64,1024]{1,0:T(8,128)(2,1)}), bf16[2048,1024]{1,0:T(8,128)(2,1)}) %all-gather.7.cloned.1.call-update) | async-done | bytes 4194320 | tf_op jit(solution)/shard_map/all_gather | solution.py:69
  106.7 10.1 %multiply_reduce_fusion = f32[1024]{0:T(1024)S(1)} fusion(f32[1024,1024]{0,1:T(8,128)} %fusion.47, bf16[1024,2048]{1,0:T(8,128)(2,1)} %param.11, bf16[2048,1024]{1,0:T(8,128)(2,1)} %all-gather.7.cloned.1.call-done, f32[1024]{0:T(1024)S(1)} %copy-done.2), kind=kOutput, calls=%fused_computation.6 | convolution fusion | flops 4302306304 | bytes 12591104 | tf_op jit(solution)/shard_map/dot_general | solution.py:47
  116.9 10.7 %all-reduce.2 = (f32[1024]{0:T(1024)S(1)}, f32[32]{0:T(128)S(1)}) all-reduce(f32[1024]{0:T(1024)S(1)} %multiply_reduce_fusion, f32[32]{0:T(128)S(1)} %convert_dynamic-update-slice_fusion), channel_id=2, replica_groups=mesh['fsdp'=32,'seq'=4] {'seq'}, use_global_device_ids=true, to_apply=%region_1.2.clone | all-reduce | flops 1056 | bytes 8448
  127.7 0.1 reduce_sum.46
  127.9 0.5 add_divide_fusion
  128.4 32.8 %all-gather.9.cloned.1.call-done = bf16[8192,512]{1,0:T(8,128)(2,1)} async-done(((bf16[256,512]{1,0:T(8,128)(2,1)}), bf16[8192,512]{1,0:T(8,128)(2,1)}) %all-gather.9.cloned.1.call-update) | async-done | bytes 8388624 | tf_op jit(solution)/shard_map/all_gather | solution.py:79
  161.2 7.0 %fusion.6 = f32[256,512]{1,0:T(8,128)S(1)} fusion(bf16[8192,512]{1,0:T(8,128)(2,1)} %all-gather.9.cloned.1.call-done, bf16[256,8192]{1,0:T(8,128)(2,1)} %param.15, f32[8192]{0:T(1024)S(1)} %copy-done.1, f32[256]{0:T(256)S(1)} %add_rsqrt_fusion), kind=kOutput, calls=%fused_computation.8 | convolution fusion | flops 2155872256 | bytes 13140992 | tf_op jit(solution)/shard_map/dot_general | solution.py:46
  168.2 0.2 reshape.54
  168.4 0.9 fusion.21
  169.3 0.7 fusion.45
  170.0 0.1 divide_bitcast_fusion
  170.1 0.5 fusion.19
  170.6 12.2 %all_gather.27 = f32[32,512]{1,0:T(8,128)S(1)} all-gather(f32[8,512]{1,0:T(8,128)S(1)} %bitcast.83), channel_id=1, replica_groups=mesh['fsdp'=32,'seq'=4] {'seq'}, dimensions={0}, use_global_device_ids=true | all-gather | bytes 81920 | tf_op jit(solution)/shard_map/all_gather | solution.py:95
  182.8 32.9 %all-gather.11.cloned.1.call-done = bf16[8192,512]{1,0:T(8,128)(2,1)} async-done(((bf16[256,512]{1,0:T(8,128)(2,1)}), bf16[8192,512]{1,0:T(8,128)(2,1)}) %all-gather.11.cloned.1.call-update) | async-done | bytes 8388624 | tf_op jit(solution)/shard_map/all_gather | solution.py:80
  215.7 7.0 %fusion.4 = f32[256,512]{1,0:T(8,128)S(1)} fusion(bf16[8192,512]{1,0:T(8,128)(2,1)} %all-gather.11.cloned.1.call-done, bf16[256,8192]{1,0:T(8,128)(2,1)} %param.15, f32[8192]{0:T(1024)S(1)} %copy-done.1, f32[256]{0:T(256)S(1)} %add_rsqrt_fusion), kind=kOutput, calls=%fused_computation.7 | convolution fusion | flops 2155872256 | bytes 13140992 | tf_op jit(solution)/shard_map/dot_general | solution.py:47
  222.7 0.2 reshape.55
  222.9 0.5 fusion.17
  223.5 12.2 %all_gather.25 = f32[32,512]{1,0:T(8,128)S(1)} all-gather(f32[8,512]{1,0:T(8,128)S(1)} %bitcast.82), channel_id=1, replica_groups=mesh['fsdp'=32,'seq'=4] {'seq'}, dimensions={0}, use_global_device_ids=true | all-gather | bytes 81920 | tf_op jit(solution)/shard_map/all_gather | solution.py:96
  235.6 0.3 fusion.46
  235.9 0.2 fusion.31
  236.1 0.9 fusion.16
  (17 shorter events, 0.4 us)
Async XLA Ops:
  7.2 5.4 %copy-start = (f32[4,4,128]{2,1,0:T(4,128)S(1)}, f32[4,4,128]{2,1,0:T(4,128)}, u32[]{:S(2)}) copy-start(f32[4,4,128]{2,1,0:T(4,128)} %param.19) | copy-start | bytes 24580
  7.2 51.8 %all-gather.5.cloned.1.call-start = ((), (), s32[]{:S(2)}) async-start(), calls=%async_computation | async-start | bytes 4325376 | tf_op jit(solution)/shard_map/all_gather | solution.py:68
  7.9 98.8 %all-gather.7.cloned.1.call-start = ((), (), s32[]{:S(2)}) async-start(), calls=%async_computation.1 | async-start | bytes 4325376 | tf_op jit(solution)/shard_map/all_gather | solution.py:69
  8.7 152.5 %all-gather.9.cloned.1.call-start = ((), (), s32[]{:S(2)}) async-start(), calls=%async_computation.2 | async-start | bytes 8650752 | tf_op jit(solution)/shard_map/all_gather | solution.py:79
  9.4 206.3 %all-gather.11.cloned.1.call-start = ((), (), s32[]{:S(2)}) async-start(), calls=%async_computation.3 | async-start | bytes 8650752 | tf_op jit(solution)/shard_map/all_gather | solution.py:80
  18.0 88.7 %copy-start.2 = (f32[1024]{0:T(1024)S(1)}, f32[1024]{0:T(1024)}, u32[]{:S(2)}) copy-start(f32[1024]{0:T(1024)} %param.14) | copy-start | bytes 12292
  69.0 92.2 %copy-start.1 = (f32[8192]{0:T(1024)S(1)}, f32[8192]{0:T(1024)}, u32[]{:S(2)}) copy-start(f32[8192]{0:T(1024)} %param.16) | copy-start | bytes 98308
Sparse Core Ops, SparseCore 0:
  10.2 48.6 all-gather.4
  61.2 45.4 all-gather.6
  109.0 52.1 all-gather.8
  163.3 52.3 all-gather.10
where the time goes:
time: 244 us; the launch traced here: 243 us
  waiting for transfers between devices  147 us (60%)
  matrix products  38.2 us (16%)
  blocking collectives  35 us (14%)
  between operations  15.2 us (6%)
  other arithmetic  6.1 us (2%)
    all_gather x1, waiting for transfers between devices, local(): lax.all_gather(draft_gate, 'fsdp', axis=0, tiled=True)  41 us
    all_gather x1, waiting for transfers between devices, local(): lax.all_gather(draft_up, 'fsdp', axis=0, tiled=True)  37.8 us
    all_gather x1, waiting for transfers between devices, local(): lax.all_gather(value_weight, 'fsdp', axis=0, tiled=True)  32.9 us
    all_gather x1, waiting for transfers between devices, local(): lax.all_gather(key_weight, 'fsdp', axis=0, tiled=True)  32.8 us
    dot_general x2, matrix products, project_pair(): jnp.dot(row_block, pieces[1], preferred_element_type=jnp.float32)  17.2 us
    dot_general x2, matrix products, project_pair(): jnp.dot(row_block, pieces[0], preferred_element_type=jnp.float32)  17 us
    all_gather x1, blocking collectives, local(): lax.all_gather(summary_value.reshape(seg_count, KVH * HD), 'seq', axis=0,...  12.2 us
    all_gather x1, blocking collectives, local(): lax.all_gather(summary_key.reshape(seg_count, KVH * HD), 'seq', axis=0, t...  12.2 us
  transfers between devices with their start and end apart: 4, of which 4 were waited for; matrix products, arithmetic and copies ran while one was open for 15% of the time, Pallas kernels for 0%

commit v1 on v0

--- a/solution.py
+++ b/solution.py
@@ -61,6 +61,15 @@
     flags,
     owner,
 ):
+
+    def group_scales(arr):
+        store = []
+        for _ in range(jax.lax.axis_size("fsdp")):
+            store.append(arr)
+        local_next = jnp.stack(store, 0)
+        last = jax.lax.all_to_all(local_next, "fsdp", split_axis=0, concat_axis=0)
+        return jnp.concatenate(last, 0)
+
     seg_count = flags.shape[0]
     gate, upward = project_pair(
         draft_tokens,
@@ -74,11 +83,7 @@
     draft_score = jnp.mean(own_scores.reshape(seg_count, SEGL), axis=1)
     normed = normalize_rows(verifier_rows, norm_gain)
     seg_keys, seg_values = project_pair(
-        normed,
-        (
-            lax.all_gather(key_weight, "fsdp", axis=0, tiled=True),
-            lax.all_gather(value_weight, "fsdp", axis=0, tiled=True),
-        ),
+        normed, (group_scales(key_weight), lax.all_gather(value_weight, "fsdp", axis=0, tiled=True))
     )
     lane_pick = (
         owner[:, None] == jnp.arange(pool_query.shape[0], dtype=jnp.int32)[None, :]

time: 244 us -> 264 us (1.082)
  local copies, waits for them, and re-layouts: 1.87 us -> 29.6 us
  waiting for transfers between devices: 147 us -> 130 us
  starting transfers between devices: 0.15 us -> 8.82 us
    all_to_all x0 -> x1, waiting for transfers between devices: none -> 104 us  [group_scales(): last = jax.lax.all_to_all(local_next, 'fsdp', split_axis=0, concat_axis=0)]
    all_gather x1, waiting for transfers between devices: 41 us -> 0.02 us  [local(): lax.all_gather(draft_gate, 'fsdp', axis=0, tiled=True)]
    all_gather x1, waiting for transfers between devices: 37.8 us -> 3.35 us  [local(): lax.all_gather(draft_up, 'fsdp', axis=0, tiled=True)]
    all_gather x1 -> x0, waiting for transfers between devices: 32.8 us -> none  [local(): lax.all_gather(key_weight, 'fsdp', axis=0, tiled=True)]
    all_gather x1, waiting for transfers between devices: 32.9 us -> 20.4 us  [local(): lax.all_gather(value_weight, 'fsdp', axis=0, tiled=True)]
    all_to_all x0 -> x1, local copies, waits for them, and re-layouts: none -> 12 us  [group_scales(): last = jax.lax.all_to_all(local_next, 'fsdp', split_axis=0, concat_axis=0)]
    dot_general x0 -> x1, local copies, waits for them, and re-layouts: none -> 11.4 us  [project_pair(): jnp.dot(row_block, pieces[0], preferred_element_type=jnp.float32)]
    all_to_all x0 -> x1, starting transfers between devices: none -> 8.71 us  [group_scales(): last = jax.lax.all_to_all(local_next, 'fsdp', split_axis=0, concat_axis=0)]
  transfers between devices with their start and end apart: 4 -> 4, of which waited for: 4 -> 3; matrix products, arithmetic and copies ran while one was open for 15% -> 25% of each run, Pallas kernels for 0% -> 0%
where the time goes in v1:
time: 264 us; the launch traced here: 263 us
  waiting for transfers between devices  130 us (49%)
  matrix products  36.7 us (14%)
  blocking collectives  34.7 us (13%)
  local copies, waits for them, and re-layouts  29.6 us (11%)
  between operations  15.2 us (6%)
  starting transfers between devices  8.82 us (3%)
  other arithmetic  8.23 us (3%)
    all_to_all x1, waiting for transfers between devices, group_scales(): last = jax.lax.all_to_all(local_next, 'fsdp', split_axis=0, concat_axis=0)  104 us
    all_gather x1, waiting for transfers between devices, local(): lax.all_gather(value_weight, 'fsdp', axis=0, tiled=True)  20.4 us
    dot_general x2, matrix products, project_pair(): jnp.dot(row_block, pieces[1], preferred_element_type=jnp.float32)  17.1 us
    dot_general x2, matrix products, project_pair(): jnp.dot(row_block, pieces[0], preferred_element_type=jnp.float32)  16.2 us
    all_gather x1, blocking collectives, local(): lax.all_gather(summary_value.reshape(seg_count, KVH * HD), 'seq', axis=0,...  12.2 us
    all_gather x1, blocking collectives, local(): lax.all_gather(summary_key.reshape(seg_count, KVH * HD), 'seq', axis=0, t...  12.1 us
    all_to_all x1, local copies, waits for them, and re-layouts, group_scales(): last = jax.lax.all_to_all(local_next, 'fsdp', split_axis=0, concat_axis=0)  12 us
    dot_general x1, local copies, waits for them, and re-layouts, project_pair(): jnp.dot(row_block, pieces[0], preferred_element_type=jnp.float32)  11.4 us
  transfers between devices with their start and end apart: 4, of which 3 were waited for; matrix products, arithmetic and copies ran while one was open for 25% of the time, Pallas kernels for 0%

profile of v1, /device:TPU:0, one launch (start us, length us, event | category | flops | bytes accessed | tf_op | source)
XLA Modules:
  0.0 262.9 jit_solution(11077858879582267644)
XLA Ops:
  7.2 0.7 all-gather.4.cloned.1.call-update
  8.0 0.7 all-gather.6.cloned.1.call-update
  8.7 0.7 all-gather.8.cloned.1.call-update
  9.4 1.1 copy.28
  10.5 4.2 %stack.2 = bf16[32,256,512]{1,2,0:T(8,128)(2,1)} broadcast(bf16[256,512]{0,1:T(8,128)(2,1)S(1)} %copy.28), dimensions={1,2} | broadcast | bytes 8650752 | tf_op jit(solution)/shard_map/stack | solution.py:69
  14.7 8.7 %all-to-all-start = ((bf16[32,256,512]{1,2,0:T(8,128)(2,1)}), bf16[32,256,512]{1,2,0:T(8,128)(2,1)}, u32[]{:S(2)}, u32[]{:S(2)}) async-start(bf16[32,256,512]{1,2,0:T(8,128)(2,1)} %stack.2), calls=%async_computation | async-start | bytes 16777216 | tf_op jit(solution)/shard_map/all_to_all | solution.py:70
  23.4 0.6 fusion.38
  25.3 0.2 convolution_bitcast_fusion.1
  25.6 3.3 %fusion.1 = f32[256]{0:T(256)S(1)} fusion(bf16[256,8192]{1,0:T(8,128)(2,1)} %param.15), kind=kLoop, calls=%fused_computation.3 | loop fusion | flops 6291200 | bytes 4195328 | tf_op jit(solution)/shard_map/reduce_sum | solution.py:15
  28.9 3.2 %fusion.3 = bf16[256,8192]{1,0:T(8,128)(2,1)} fusion(bf16[256,8192]{1,0:T(8,128)(2,1)S(1)} %copy-done.2, f32[8192]{0:T(1024)S(1)} %copy-done.3, f32[256]{0:T(256)S(1)} %add_rsqrt_fusion), kind=kLoop, calls=%fused_computation.5 | loop fusion | flops 8388608 | bytes 8422400 | tf_op jit(solution)/shard_map/convert_element_type | solution.py:16
  32.2 103.9 %all-to-all-done = bf16[32,256,512]{1,2,0:T(8,128)(2,1)} async-done(((bf16[32,256,512]{1,2,0:T(8,128)(2,1)}), bf16[32,256,512]{1,2,0:T(8,128)(2,1)}, u32[]{:S(2)}, u32[]{:S(2)}) %all-to-all-start) | async-done | bytes 8388640 | tf_op jit(solution)/shard_map/all_to_all | solution.py:70
  136.0 12.0 %copy.29 = bf16[32,256,512]{2,1,0:T(8,128)(2,1)} copy(bf16[32,256,512]{1,2,0:T(8,128)(2,1)} %all-to-all-done) | data formatting | bytes 16777216 | tf_op jit(solution)/shard_map/all_to_all | solution.py:70
  148.0 11.4 %copy.30 = bf16[512,8192]{1,0:T(8,128)(2,1)} copy(bf16[512,8192]{0,1:T(8,128)(2,1)} %bitcast.97) | data formatting | bytes 16777216 | tf_op jit(solution)/shard_map/dot_general | solution.py:46
  159.4 6.1 %fusion.42 = f32[8,32,4,128]{3,1,2,0:T(8,128)S(1)} fusion(bf16[8,32,8192,1]{2,1,3,0:T(8,128)(2,1)} %bitcast.99, bf16[4,128,8192,1]{2,1,0,3:T(8,128)(2,1)} %bitcast.98), kind=kOutput, calls=%fused_computation.60 | convolution fusion | flops 2147483648 | bytes 13107200 | tf_op jit(solution)/shard_map/dot_general | solution.py:46
  165.5 0.9 fusion.21
  166.4 0.7 fusion.39
  167.2 0.5 fusion.25
  167.8 10.1 %fusion.41 = f32[1024,1024]{0,1:T(8,128)} fusion(bf16[1024,2048]{1,0:T(8,128)(2,1)} %param.11, bf16[2048,1024]{1,0:T(8,128)(2,1)} %all-gather.4.cloned.1.call-done), kind=kOutput, calls=%fused_computation.59 | convolution fusion | flops 4294967296 | bytes 12582912 | tf_op jit(solution)/shard_map/dot_general | solution.py:46
  177.9 3.3 %all-gather.6.cloned.1.call-done = bf16[2048,1024]{1,0:T(8,128)(2,1)} async-done(((bf16[64,1024]{1,0:T(8,128)(2,1)}), bf16[2048,1024]{1,0:T(8,128)(2,1)}) %all-gather.6.cloned.1.call-update) | async-done | bytes 4194320 | tf_op jit(solution)/shard_map/all_gather | solution.py:78
  181.3 10.1 %multiply_reduce_fusion = f32[1024]{0:T(1024)S(1)} fusion(f32[1024,1024]{0,1:T(8,128)} %fusion.41, bf16[1024,2048]{1,0:T(8,128)(2,1)} %param.11, bf16[2048,1024]{1,0:T(8,128)(2,1)} %all-gather.6.cloned.1.call-done, f32[1024]{0:T(1024)S(1)} %copy-done.6), kind=kOutput, calls=%fused_computation.6 | convolution fusion | flops 4302306304 | bytes 12591104 | tf_op jit(solution)/shard_map/dot_general | solution.py:47
  191.4 10.4 %all-reduce.2 = (f32[1024]{0:T(1024)S(1)}, f32[32]{0:T(128)S(1)}) all-reduce(f32[1024]{0:T(1024)S(1)} %multiply_reduce_fusion, f32[32]{0:T(128)S(1)} %convert_dynamic-update-slice_fusion), channel_id=2, replica_groups=mesh['fsdp'=32,'seq'=4] {'seq'}, use_global_device_ids=true, to_apply=%region_1.2.clone | all-reduce | flops 1056 | bytes 8448
  202.0 0.1 reduce_sum.46
  202.1 12.1 %all_gather.23 = f32[32,512]{1,0:T(8,128)S(1)} all-gather(f32[8,512]{1,0:T(8,128)S(1)} %bitcast.100), channel_id=1, replica_groups=mesh['fsdp'=32,'seq'=4] {'seq'}, dimensions={0}, use_global_device_ids=true | all-gather | bytes 81920 | tf_op jit(solution)/shard_map/all_gather | solution.py:100
  214.2 0.3 fusion.40
  214.5 0.2 fusion.24
  214.7 0.5 add_divide_fusion
  215.2 20.4 %all-gather.8.cloned.1.call-done = bf16[8192,512]{1,0:T(8,128)(2,1)} async-done(((bf16[256,512]{1,0:T(8,128)(2,1)}), bf16[8192,512]{1,0:T(8,128)(2,1)}) %all-gather.8.cloned.1.call-update) | async-done | bytes 8388624 | tf_op jit(solution)/shard_map/all_gather | solution.py:86
  235.6 7.0 %fusion.43 = f32[256,512]{1,0:T(8,128)S(1)} fusion(bf16[256,8192]{1,0:T(8,128)(2,1)} %fusion.3, bf16[8192,512]{1,0:T(8,128)(2,1)} %all-gather.8.cloned.1.call-done), kind=kOutput, calls=%fused_computation.61 | convolution fusion | flops 2147483648 | bytes 13107200 | tf_op jit(solution)/shard_map/dot_general | solution.py:47
  242.6 0.2 reshape.60
  242.8 0.5 fusion.13
  243.3 12.2 %all_gather.21 = f32[32,512]{1,0:T(8,128)S(1)} all-gather(f32[8,512]{1,0:T(8,128)S(1)} %bitcast.101), channel_id=1, replica_groups=mesh['fsdp'=32,'seq'=4] {'seq'}, dimensions={0}, use_global_device_ids=true | all-gather | bytes 81920 | tf_op jit(solution)/shard_map/all_gather | solution.py:101
  255.5 0.8 fusion.12
  (30 shorter events, 0.5 us)
Async XLA Ops:
  7.2 18.1 %copy-start = (f32[4,4,128]{2,1,0:T(4,128)S(1)}, f32[4,4,128]{2,1,0:T(4,128)}, u32[]{:S(2)}) copy-start(f32[4,4,128]{2,1,0:T(4,128)} %param.19) | copy-start | bytes 24580
  7.2 160.6 %all-gather.4.cloned.1.call-start = ((), (), s32[]{:S(2)}) async-start(), calls=%async_computation.1 | async-start | bytes 4325376 | tf_op jit(solution)/shard_map/all_gather | solution.py:77
  7.9 173.4 %all-gather.6.cloned.1.call-start = ((), (), s32[]{:S(2)}) async-start(), calls=%async_computation.2 | async-start | bytes 4325376 | tf_op jit(solution)/shard_map/all_gather | solution.py:78
  8.7 226.9 %all-gather.8.cloned.1.call-start = ((), (), s32[]{:S(2)}) async-start(), calls=%async_computation.3 | async-start | bytes 8650752 | tf_op jit(solution)/shard_map/all_gather | solution.py:86
  14.7 8.7 %copy-start.4 = (u32[128]{0:T(128)S(1)}, u32[128]{0:T(128)}, u32[]{:S(2)}) copy-start(u32[128]{0:T(128)} %constant.31) | copy-start | bytes 1540
  14.7 10.6 %copy-start.5 = (s32[8]{0:T(128)S(1)}, s32[8]{0:T(128)}, u32[]{:S(2)}) copy-start(s32[8]{0:T(128)} %param.21) | copy-start | bytes 100
  14.7 10.9 %copy-start.7 = (s32[8]{0:T(128)S(1)}, s32[8]{0:T(128)}, u32[]{:S(2)}) copy-start(s32[8]{0:T(128)} %param.20) | copy-start | bytes 100
  14.7 121.4 %all-to-all-start = ((bf16[32,256,512]{1,2,0:T(8,128)(2,1)}), bf16[32,256,512]{1,2,0:T(8,128)(2,1)}, u32[]{:S(2)}, u32[]{:S(2)}) async-start(bf16[32,256,512]{1,2,0:T(8,128)(2,1)} %stack.2), calls=%async_computation | async-start | bytes 16777216 | tf_op jit(solution)/shard_map/all_to_all | solution.py:70
  23.4 5.6 %copy-start.3 = (f32[8192]{0:T(1024)S(1)}, f32[8192]{0:T(1024)}, u32[]{:S(2)}) copy-start(f32[8192]{0:T(1024)} %param.16) | copy-start | bytes 98308
  25.3 3.6 %copy-start.2 = (bf16[256,8192]{1,0:T(8,128)(2,1)S(1)}, bf16[256,8192]{1,0:T(8,128)(2,1)}, u32[]{:S(2)}) copy-start(bf16[256,8192]{1,0:T(8,128)(2,1)} %param.15) | copy-start | bytes 12582916
  167.8 13.5 %copy-start.6 = (f32[1024]{0:T(1024)S(1)}, f32[1024]{0:T(1024)}, u32[]{:S(2)}) copy-start(f32[1024]{0:T(1024)} %param.14) | copy-start | bytes 12292
  235.6 20.7 %copy-start.1 = (f32[4,4,128]{2,1,0:T(4,128)S(1)}, f32[4,4,128]{2,1,0:T(4,128)}, u32[]{:S(2)}) copy-start(f32[4,4,128]{2,1,0:T(4,128)} %param.19) | copy-start | bytes 24580
Sparse Core Ops, SparseCore 0:
  10.3 116.5 all-gather.3
  129.1 52.0 all-gather.5
  183.5 52.0 all-gather.7
